TPU v7x, 32 devices: a whole 2x2x4 slice. The times are simulated.
32 devices in a mesh: row: 2 (over x), col: 4 (over z), tok: 4 (over y, core).
Axes of the slice: x: 2, y: 2, z: 4, core: 2. Of those that a mesh axis runs over, the one named last changes fastest.
Arguments:
- activations: bfloat16 [4096, 2048], P(('row', 'col', 'tok')), may hold values from -6 to 6
- norm_gain: float32 [2048], replicated, may hold values from 0.1 to 1.9
- routes: int32 [4096, 8], P(('row', 'col', 'tok')), may hold values from 0 to 127, all different within a row; in each aligned block of 128 rows (0 to 127, 128 to 255, ...) at most 10 rows name the same one
- route_weights: float32 [4096, 8], P(('row', 'col', 'tok')), may hold values from 0.05 to 1
- gate_up_weight: bfloat16 [128, 2, 768, 2048], P(('row', 'col'), None, 'tok'), may hold values from -0.125 to 0.125
- down_weight: bfloat16 [128, 768, 2048], P(('row', 'col'), 'tok'), may hold values from -0.21875 to 0.21875
Outputs:
- expert_mix: bfloat16 [4096, 2048], P(('row', 'col', 'tok'))
Inputs may be any that keep to these rules, and one draw needn't show every extreme that they name: `routes`: within the rows of one device no expert is named by more than 10 rows, a bound that some block reaches.
All inputs are finite; a program needn't handle non-finite values.
Results may differ from a plain program's by a relative error of at most 0.0085.
Values may be sent and summed in bfloat16 or wider, within the bound.
No kernel may reach another device: no remote copies, remote signals or barrier semaphores. Data moves between devices by JAX's collectives and lax.ppermute only.
A program may use at most 384 MiB of HBM per device.

v0:
```python
import jax
import jax.numpy as jnp
from jax import lax
from jax.sharding import PartitionSpec as P

CAP = 10
EPSILON = 1e-06


def rank_in_block(block_routes, experts):
    onehot = (block_routes[:, None] == jnp.arange(experts, dtype=jnp.int32)[None, :]).astype(
        jnp.int32
    )
    before = jnp.cumsum(onehot, axis=0) - onehot
    return jnp.sum(before * onehot, axis=1)


def rms_normed(activations, norm_gain):
    values = activations.astype(jnp.float32)
    scale = lax.rsqrt(jnp.mean(values * values, axis=-1, keepdims=True) + EPSILON)
    return (values * scale * norm_gain).astype(jnp.bfloat16)


def apply_experts(received, gate_up_weight, down_weight):
    both = jnp.einsum(
        "sjcd,jgfd->sjcgf",
        received,
        lax.all_gather(gate_up_weight, "tok", axis=2, tiled=True),
        preferred_element_type=jnp.float32,
    )
    hidden = (jax.nn.silu(both[:, :, :, 0, :]) * both[:, :, :, 1, :]).astype(jnp.bfloat16)
    summed = jnp.einsum(
        "sjcf,jfd->sjcd",
        hidden,
        lax.all_gather(down_weight, "tok", axis=1, tiled=True),
        preferred_element_type=jnp.float32,
    )
    return summed.astype(jnp.bfloat16)


def local(activations, norm_gain, routes, route_weights, gate_up_weight, down_weight):
    count, features = activations.shape
    chosen = routes.shape[1]
    holding = gate_up_weight.shape[0]
    row_count = lax.axis_size("row")
    col_count = lax.axis_size("col")
    owners = row_count * col_count
    experts = holding * owners
    normed = rms_normed(activations, norm_gain)
    gates = route_weights / jnp.sum(route_weights, axis=1, keepdims=True)
    flat_routes = routes.reshape(-1)
    target = flat_routes * CAP + rank_in_block(flat_routes, experts)
    token_ids = jnp.arange(count * chosen, dtype=jnp.int32) // chosen
    source = jnp.full((experts * CAP,), count, jnp.int32).at[target].set(token_ids)
    outbound = jnp.take(normed, source, axis=0, mode="fill", fill_value=0)
    outbound = outbound.reshape(owners, holding, CAP, features)
    arrived = lax.all_to_all(outbound, ("row", "col"), split_axis=0, concat_axis=0, tiled=True)
    results = apply_experts(arrived, gate_up_weight, down_weight)
    returned = lax.all_to_all(results, ("row", "col"), split_axis=0, concat_axis=0, tiled=True)
    picked = jnp.take(returned.reshape(experts * CAP, features), target, axis=0)
    picked = picked.reshape(count, chosen, features)
    mixed = jnp.einsum("tk,tkd->td", gates, picked.astype(jnp.float32))
    return mixed.astype(jnp.bfloat16)


def solution(mesh):
    in_specs = (
        P(("row", "col", "tok"), None),
        P(),
        P(("row", "col", "tok"), None),
        P(("row", "col", "tok"), None),
        P(("row", "col"), None, "tok", None),
        P(("row", "col"), "tok", None),
    )
    out_specs = P(("row", "col", "tok"), None)
    return jax.shard_map(local, mesh=mesh, in_specs=in_specs, out_specs=out_specs, check_vma=False)
```

profile of v0, /device:TPU:0, one launch (start us, length us, event | category | flops | bytes accessed | tf_op | source)
XLA Modules:
  0.0 1096.7 jit_solution(4971576280621673986)
XLA Ops:
  6.5 0.7 all-gather.3.cloned.1.call-update
  7.3 0.7 all-gather.5.cloned.1.call-update
  8.4 0.2 fusion.24
  9.1 0.4 fusion.23
  9.5 0.6 copy-done.1
  10.0 4.3 scatter_custom_fusion
  14.6 0.2 fusion.21
  14.8 6.2 gather_fusion
  21.0 10.5 gather.13
  31.8 12.9 %broadcast_select_fusion = bf16[8,16,10,2048]{3,2,1,0:T(8,128)(2,1)} fusion(bf16[8,16,10,2048]{3,2,1,0:T(8,128)(2,1)} %gather.13, pred[8,16,10]{2,1,0:T(8,128)(4,1)S(1)} %broadcast_in_dim.34), kind=kLoop, calls=%fused_computation.9 | loop fusion | flops 2621440 | bytes 10487040 | tf_op jit(solution)/shard_map/jit(_take)/select_n | solution.py:55
  44.6 8.0 copy.35
  52.6 123.2 %all_to_all.10 = bf16[8,16,10,2048]{3,1,2,0:T(8,128)(2,1)} all-to-all(bf16[8,16,10,2048]{3,1,2,0:T(8,128)(2,1)S(1)} %copy.35), channel_id=1, replica_groups=mesh['row'=2,'col'=4,'tok'=4] {'row','col'}, dimensions={0} | all-to-all | bytes 10485760 | tf_op jit(solution)/shard_map/all_to_all | solution.py:57
  175.9 421.0 %all-gather.3.cloned.1.call-done = bf16[16,2,768,2048]{3,2,1,0:T(8,128)(2,1)} async-done(((bf16[16,2,192,2048]{3,2,1,0:T(8,128)(2,1)}), bf16[16,2,768,2048]{3,2,1,0:T(8,128)(2,1)}) %all-gather.3.cloned.1.call-update) | async-done | bytes 100663312 | tf_op jit(solution)/shard_map/all_gather | solution.py:28
  596.9 58.9 %fusion.9 = f32[8,16,10,2,768]{4,2,3,0,1:T(8,128)} fusion(bf16[16,2,768,2048]{3,2,1,0:T(8,128)(2,1)} %all-gather.3.cloned.1.call-done, bf16[8,16,10,2048,1]{3,1,2,0,4:T(8,128)(2,1)} %bitcast.54), kind=kOutput, calls=%fused_computation.14 | convolution fusion | flops 8053063680 | bytes 113770496 | tf_op jit(solution)/shard_map/sjcd,jgfd->sjcgf/dot_general | solution.py:25
  655.8 241.6 %all-gather.5.cloned.1.call-done = bf16[16,768,2048]{2,1,0:T(8,128)(2,1)} async-done(((bf16[16,192,2048]{2,1,0:T(8,128)(2,1)}), bf16[16,768,2048]{2,1,0:T(8,128)(2,1)}) %all-gather.5.cloned.1.call-update) | async-done | bytes 50331664 | tf_op jit(solution)/shard_map/all_gather | solution.py:35
  897.5 24.4 %convert_bitcast_fusion = bf16[8,16,10,2048]{3,2,0,1:T(8,128)(2,1)} fusion(bf16[16,768,2048]{2,1,0:T(8,128)(2,1)} %all-gather.5.cloned.1.call-done, f32[8,16,10,2,768]{4,2,3,0,1:T(8,128)} %fusion.9), kind=kOutput, calls=%fused_computation.8 | convolution fusion | flops 4035051520 | bytes 63438848 | tf_op jit(solution)/shard_map/sjcf,jfd->sjcd/dot_general | solution.py:32
  921.9 9.1 copy.38
  931.0 5.6 all-to-all-start.1
  937.1 116.6 %all-to-all-done.1 = bf16[8,16,10,2048]{3,1,2,0:T(8,128)(2,1)} async-done(((bf16[8,16,10,2048]{3,1,2,0:T(8,128)(2,1)}), bf16[8,16,10,2048]{3,1,2,0:T(8,128)(2,1)}, u32[]{:S(2)}, u32[]{:S(2)}) %all-to-all-start.1) | async-done | bytes 5242912 | tf_op jit(solution)/shard_map/all_to_all | solution.py:59
  1053.6 9.7 copy.39
  1063.4 9.8 reshape.89
  1073.2 12.0 %gather_fusion.1 = bf16[1024,2048]{1,0:T(8,128)(2,1)} fusion(bf16[1280,2048]{1,0:T(8,128)(2,1)} %reshape.89, s32[1024]{0:T(1024)S(1)} %broadcast_clamp_fusion), kind=kCustom, calls=%fused_computation.1 | custom fusion | bytes 8392704 | tf_op jit(solution)/shard_map/jit(_take)/gather | solution.py:60
  1085.2 3.5 fusion.14
  1088.7 1.1 copy.53
  (47 shorter events, 1.7 us)
Async XLA Ops:
  6.5 590.4 %all-gather.3.cloned.1.call-start = ((), (), s32[]{:S(2)}) async-start(), calls=%async_computation.2 | async-start | bytes 125829120 | tf_op jit(solution)/shard_map/all_gather | solution.py:28
  7.3 0.8 copy-start.3
  7.3 7.1 copy-start
  7.3 7.3 copy-start.8
  7.3 890.2 %all-gather.5.cloned.1.call-start = ((), (), s32[]{:S(2)}) async-start(), calls=%async_computation.3 | async-start | bytes 62914560 | tf_op jit(solution)/shard_map/all_gather | solution.py:35
  9.4 0.6 copy-start.1
  10.0 4.3 copy-start.5
  930.9 5.6 copy-start.2
  930.9 5.8 copy-start.4
  930.9 5.9 copy-start.7
  930.9 6.1 copy-start.6
  931.0 122.7 %all-to-all-start.1 = ((bf16[8,16,10,2048]{3,1,2,0:T(8,128)(2,1)}), bf16[8,16,10,2048]{3,1,2,0:T(8,128)(2,1)}, u32[]{:S(2)}, u32[]{:S(2)}) async-start(bf16[8,16,10,2048]{3,1,2,0:T(8,128)(2,1)} %copy.38), calls=%async_computation.1 | async-start | bytes 10485760 | tf_op jit(solution)/shard_map/all_to_all | solution.py:59
Sparse Core Ops, SparseCore 0:
  8.9 587.9 all-gather.2
  598.5 298.9 all-gather.4
where the time goes:
time: 1100 us
  waiting for transfers between devices  781 us (71%)
  blocking collectives  123 us (11%)
  matrix products  86.8 us (8%)
  local copies, waits for them, and re-layouts  72.7 us (7%)
  other arithmetic  14 us (1%)
  between operations  13.6 us (1%)
    all_gather x1, waiting for transfers between devices, apply_experts(): lax.all_gather(gate_up_weight, 'tok', axis=2, tiled=True)  421 us
    all_gather x1, waiting for transfers between devices, apply_experts(): lax.all_gather(down_weight, 'tok', axis=1, tiled=True)  242 us
    all_to_all x1, blocking collectives, local(): lax.all_to_all(outbound, ('row', 'col'), split_axis=0, concat_axis=0, til...  123 us
    all_to_all x1, waiting for transfers between devices, local(): lax.all_to_all(results, ('row', 'col'), split_axis=0, concat_axis=0, tile...  117 us
    dot_general x1, matrix products, apply_experts(): jnp.einsum('sjcd,jgfd->sjcgf', received, lax.all_gather(gate_up_weight, '...  58.9 us
    dot_general x1, matrix products, apply_experts(): jnp.einsum('sjcf,jfd->sjcd', hidden, lax.all_gather(down_weight, 'tok', a...  24.4 us
  transfers between devices with their start and end apart: 3, of which 3 were waited for; matrix products, arithmetic and copies ran while one was open for 9% of the time, Pallas kernels for 0%

commit v1 on v0

--- a/solution.py
+++ b/solution.py
@@ -5,6 +5,22 @@
 
 CAP = 10
 EPSILON = 1e-06
+
+
+def product_in_turn(x, axis, dim, product):
+    devices, mine, rows = (lax.axis_size(axis), lax.axis_index(axis), x.shape[dim])
+    upward = [(i, (i + 1) % devices) for i in range(devices)]
+    backward = [(i, (i - 1) % devices) for i in range(devices)]
+    half = devices // 2
+    from_left = from_right = x
+    so_far = product(x, mine * rows)
+    for step in range(1, half + 1):
+        from_left = lax.ppermute(from_left, axis, upward)
+        if step < devices - half:
+            from_right = lax.ppermute(from_right, axis, backward)
+            so_far = so_far + product(from_right, (mine + step) % devices * rows)
+        so_far = so_far + product(from_left, (mine - step) % devices * rows)
+    return so_far
 
 
 def rank_in_block(block_routes, experts):
@@ -29,11 +45,16 @@
         preferred_element_type=jnp.float32,
     )
     hidden = (jax.nn.silu(both[:, :, :, 0, :]) * both[:, :, :, 1, :]).astype(jnp.bfloat16)
-    summed = jnp.einsum(
-        "sjcf,jfd->sjcd",
-        hidden,
-        lax.all_gather(down_weight, "tok", axis=1, tiled=True),
-        preferred_element_type=jnp.float32,
+    summed = product_in_turn(
+        down_weight,
+        "tok",
+        1,
+        lambda own_block, at: jnp.einsum(
+            "sjcf,jfd->sjcd",
+            lax.dynamic_slice_in_dim(hidden, at, own_block.shape[1], axis=3),
+            own_block,
+            preferred_element_type=jnp.float32,
+        ),
     )
     return summed.astype(jnp.bfloat16)
 

time: 1100 us -> 1250 us (1.14)
  waiting for transfers between devices: 781 us -> 1010 us
  blocking collectives: 123 us -> 0 us
  matrix products: 86.8 us -> 113 us
  starting transfers between devices: 5.67 us -> 20.6 us
    ppermute x0 -> x3, waiting for transfers between devices: none -> 360 us  [the longest x2 360 us: product_in_turn(): from_left = lax.ppermute(from_left, axis, upward)]
    all_gather x1 -> x0, waiting for transfers between devices: 242 us -> none  [apply_experts(): lax.all_gather(down_weight, 'tok', axis=1, tiled=True)]
    all_to_all x1 -> x0, blocking collectives: 123 us -> none  [local(): lax.all_to_all(outbound, ('row', 'col'), split_axis=0, concat_axis=0, til...]
    all_gather x1, waiting for transfers between devices: 421 us -> 531 us  [apply_experts(): lax.all_gather(gate_up_weight, 'tok', axis=2, tiled=True)]
    dot_general x1 -> x4, matrix products: 24.4 us -> 60.5 us  [apply_experts(): jnp.einsum('sjcf,jfd->sjcd', lax.dynamic_slice_in_dim(hidden, at, own_blo...]
  transfers between devices with their start and end apart: 3 -> 6, of which waited for: 3 -> 3; matrix products, arithmetic and copies ran while one was open for 9% -> 11% of each run, Pallas kernels for 0% -> 0%
where the time goes in v1:
time: 1250 us
  waiting for transfers between devices  1010 us (81%)
  matrix products  113 us (9%)
  local copies, waits for them, and re-layouts  72.7 us (6%)
  starting transfers between devices  20.6 us (2%)
  other arithmetic  20 us (2%)
  between operations  13.6 us (1%)
    all_gather x1, waiting for transfers between devices, apply_experts(): lax.all_gather(gate_up_weight, 'tok', axis=2, tiled=True)  531 us
    ppermute x2, waiting for transfers between devices, product_in_turn(): from_left = lax.ppermute(from_left, axis, upward)  360 us
    all_to_all x1, waiting for transfers between devices, local(): lax.all_to_all(results, ('row', 'col'), split_axis=0, concat_axis=0, tile...  116 us
    dot_general x4, matrix products, apply_experts(): jnp.einsum('sjcf,jfd->sjcd', lax.dynamic_slice_in_dim(hidden, at, own_blo...  60.5 us
    dot_general x1, matrix products, apply_experts(): jnp.einsum('sjcd,jgfd->sjcgf', received, lax.all_gather(gate_up_weight, '...  48.9 us
  transfers between devices with their start and end apart: 6, of which 3 were waited for; matrix products, arithmetic and copies ran while one was open for 11% of the time, Pallas kernels for 0%

profile of v1, /device:TPU:0, one launch (start us, length us, event | category | flops | bytes accessed | tf_op | source)
XLA Modules:
  0.0 1248.1 jit_solution(1133546867489938162)
XLA Ops:
  9.7 4.3 scatter_custom_fusion
  14.5 6.1 gather_fusion
  20.6 10.5 gather.13
  31.3 13.0 %broadcast_select_fusion = bf16[8,16,10,2048]{3,2,1,0:T(8,128)(2,1)} fusion(bf16[8,16,10,2048]{3,2,1,0:T(8,128)(2,1)} %gather.13, pred[8,16,10]{2,1,0:T(8,128)(4,1)S(1)} %broadcast_in_dim.34), kind=kLoop, calls=%fused_computation.16 | loop fusion | flops 2621440 | bytes 10487040 | tf_op jit(solution)/shard_map/jit(_take)/select_n | solution.py:76
  44.3 12.0 copy.35
  56.3 6.3 all-to-all-start
  62.6 1.3 collective-permute-start
  63.9 360.0 %collective-permute-done.1 = bf16[16,192,2048]{2,1,0:T(8,128)(2,1)} collective-permute-done((bf16[16,192,2048]{2,1,0:T(8,128)(2,1)}, bf16[16,192,2048]{2,1,0:T(8,128)(2,1)}, u32[]{:S(2)}, u32[]{:S(2)}) %collective-permute-start.1) | collective-permute-done | bytes 12582944 | tf_op jit(solution)/shard_map/ppermute | solution.py:18
  423.9 5.7 collective-permute-start.2
  429.6 531.3 %all-gather.2.cloned.1.call-done = bf16[16,2,768,2048]{3,2,1,0:T(8,128)(2,1)} async-done(((bf16[16,2,192,2048]{3,2,1,0:T(8,128)(2,1)}), bf16[16,2,768,2048]{3,2,1,0:T(8,128)(2,1)}) %all-gather.2.cloned.1.call-update) | async-done | bytes 100663312 | tf_op jit(solution)/shard_map/all_gather | solution.py:44
  960.9 48.9 %fusion.14 = f32[8,16,10,2,768]{4,2,3,0,1:T(8,128)} fusion(bf16[16,2,768,2048]{3,2,1,0:T(8,128)(2,1)} %all-gather.2.cloned.1.call-done, bf16[8,16,10,2048,1]{3,1,2,0,4:T(8,128)(2,1)} %bitcast.6), kind=kOutput, calls=%fused_computation.21 | convolution fusion | flops 8053063680 | bytes 113770496 | tf_op jit(solution)/shard_map/sjcd,jgfd->sjcgf/dot_general | solution.py:41
  1009.8 5.9 fusion.13
  1015.7 13.9 %fusion.8 = f32[16,8,10,2048]{3,2,1,0:T(8,128)} fusion(bf16[16,192,2048]{2,1,0:T(8,128)(2,1)} %param.11, bf16[8,16,10,768]{3,2,0,1:T(8,128)(2,1)S(1)} %fusion.13, s32[]{:T(128)S(6)} %select_n.69), kind=kOutput, calls=%fused_computation.12 | convolution fusion | flops 1006632960 | bytes 24117252 | tf_op jit(solution)/shard_map/sjcf,jfd->sjcd/dot_general | solution.py:52
  1029.5 12.7 %fusion.4 = f32[16,8,10,2048]{3,2,1,0:T(8,128)} fusion(bf16[16,192,2048]{2,1,0:T(8,128)(2,1)} %collective-permute-done.1, bf16[8,16,10,768]{3,2,0,1:T(8,128)(2,1)S(1)} %fusion.13, s32[]{:T(128)S(6)} %select_n.73), kind=kOutput, calls=%fused_computation.8 | convolution fusion | flops 1006632960 | bytes 24117252 | tf_op jit(solution)/shard_map/sjcf,jfd->sjcd/dot_general | solution.py:52
  1042.2 12.7 %fusion.6 = f32[16,8,10,2048]{3,2,1,0:T(8,128)} fusion(bf16[16,192,2048]{2,1,0:T(8,128)(2,1)} %collective-permute-done, bf16[8,16,10,768]{3,2,0,1:T(8,128)(2,1)S(1)} %fusion.13, s32[]{:T(128)S(6)} %select_n.71), kind=kOutput, calls=%fused_computation.10 | convolution fusion | flops 1006632960 | bytes 24117252 | tf_op jit(solution)/shard_map/sjcf,jfd->sjcd/dot_general | solution.py:52
  1055.0 21.2 %fusion.10 = bf16[8,16,10,2048]{3,2,0,1:T(8,128)(2,1)S(1)} fusion(f32[16,8,10,2048]{3,2,1,0:T(8,128)} %fusion.4, f32[16,8,10,2048]{3,2,1,0:T(8,128)} %fusion.8, f32[16,8,10,2048]{3,2,1,0:T(8,128)} %fusion.6, bf16[16,192,2048]{2,1,0:T(8,128)(2,1)} %collective-permute-done.2, bf16[8,16,10,768]{3,2,0,1:T(8,128)(2,1)} %copy-done, s32[]{:T(128)S(6)} %select_n.75), kind=kOutput, calls=%fused_computation.14 | convolution fusion | flops 1017118720 | bytes 69206016 | tf_op jit(solution)/shard_map/sjcf,jfd->sjcd/dot_general | solution.py:52
  1076.1 5.3 copy.38
  1081.5 6.7 all-to-all-start.1
  1088.7 116.4 %all-to-all-done.1 = bf16[8,16,10,2048]{3,1,2,0:T(8,128)(2,1)} async-done(((bf16[8,16,10,2048]{3,1,2,0:T(8,128)(2,1)}), bf16[8,16,10,2048]{3,1,2,0:T(8,128)(2,1)}, u32[]{:S(2)}, u32[]{:S(2)}) %all-to-all-start.1) | async-done | bytes 5242912 | tf_op jit(solution)/shard_map/all_to_all | solution.py:80
  1205.2 9.7 copy.39
  1214.9 9.8 reshape.89
  1224.7 12.0 gather_fusion.1
  1236.7 3.5 fusion.19
  1240.2 1.1 copy.56
  (57 shorter events, 4.2 us)
Async XLA Ops:
  6.5 1.2 copy-start.4
  6.5 7.6 copy-start.1
  6.5 7.8 copy-start.9
  6.5 954.3 %all-gather.2.cloned.1.call-start = ((), (), s32[]{:S(2)}) async-start(), calls=%async_computation.2 | async-start | bytes 125829120 | tf_op jit(solution)/shard_map/all_gather | solution.py:44
  7.3 416.6 %collective-permute-start.1 = (bf16[16,192,2048]{2,1,0:T(8,128)(2,1)}, bf16[16,192,2048]{2,1,0:T(8,128)(2,1)}, u32[]{:S(2)}, u32[]{:S(2)}) collective-permute-start(bf16[16,192,2048]{2,1,0:T(8,128)(2,1)} %param.11), channel_id=1, source_target_pairs={{0,1},{1,2},{2,3},{3,0},{4,5},{5,6},{6,7},{7,4},{8,9},{9,10},{10,1... | collective-permute-start | bytes 37748744 | tf_op jit(solution)/shard_map/ppermute | solution.py:18
  9.1 0.6 copy-start.2
  9.7 4.3 copy-start.6
  56.3 373.3 %all-to-all-start = ((bf16[8,16,10,2048]{3,1,2,0:T(8,128)(2,1)}), bf16[8,16,10,2048]{3,1,2,0:T(8,128)(2,1)}, u32[]{:S(2)}, u32[]{:S(2)}) async-start(bf16[8,16,10,2048]{3,1,2,0:T(8,128)(2,1)} %copy.35), calls=%async_computation | async-start | bytes 10485760 | tf_op jit(solution)/shard_map/all_to_all | solution.py:78
  62.6 979.6 %collective-permute-start = (bf16[16,192,2048]{2,1,0:T(8,128)(2,1)}, bf16[16,192,2048]{2,1,0:T(8,128)(2,1)}, u32[]{:S(2)}, u32[]{:S(2)}) collective-permute-start(bf16[16,192,2048]{2,1,0:T(8,128)(2,1)} %param.11), channel_id=1, source_target_pairs={{0,3},{1,0},{2,1},{3,2},{4,7},{5,4},{6,5},{7,6},{8,11},{9,8},{10,9... | collective-permute-start | bytes 37748744 | tf_op jit(solution)/shard_map/ppermute | solution.py:20
  423.9 631.1 %collective-permute-start.2 = (bf16[16,192,2048]{2,1,0:T(8,128)(2,1)}, bf16[16,192,2048]{2,1,0:T(8,128)(2,1)}, u32[]{:S(2)}, u32[]{:S(2)}) collective-permute-start(bf16[16,192,2048]{2,1,0:T(8,128)(2,1)} %collective-permute-done.1), channel_id=1, source_target_pairs={{0,1},{1,2},{2,3},{3,0},{4,5},{5,6},{6,7},{7,4},{8,9},{9,10},{10,1... | collective-permute-start | bytes 37748744 | tf_op jit(solution)/shard_map/ppermute | solution.py:18
  1015.7 26.6 %copy-start = (bf16[8,16,10,768]{3,2,0,1:T(8,128)(2,1)}, bf16[8,16,10,768]{3,2,0,1:T(8,128)(2,1)S(1)}, u32[]{:S(2)}) copy-start(bf16[8,16,10,768]{3,2,0,1:T(8,128)(2,1)S(1)} %fusion.13) | copy-start | bytes 5898244
  1081.5 6.7 copy-start.3
  1081.5 6.9 copy-start.5
  1081.5 7.0 copy-start.8
  1081.5 7.2 copy-start.7
  1081.5 123.7 %all-to-all-start.1 = ((bf16[8,16,10,2048]{3,1,2,0:T(8,128)(2,1)}), bf16[8,16,10,2048]{3,1,2,0:T(8,128)(2,1)}, u32[]{:S(2)}, u32[]{:S(2)}) async-start(bf16[8,16,10,2048]{3,1,2,0:T(8,128)(2,1)} %copy.38), calls=%async_computation.1 | async-start | bytes 10485760 | tf_op jit(solution)/shard_map/all_to_all | solution.py:80
Sparse Core Ops, SparseCore 0:
  8.9 951.8 all-gather.1
